TPU v7x, 512 devices: a whole 4x4x16 slice. The times are simulated.
512 devices in a mesh: clus: 128 (over x, z, core), sub: 4 (over y).
Axes of the slice: x: 4, y: 4, z: 16, core: 2. Of those that a mesh axis runs over, the one named last changes fastest.
Arguments:
- residual_in: float32 [2048, 32, 512], P(('clus', 'sub')), may hold values from -6 to 6
- local_inverse: bfloat16 [2048, 512, 512], P(('clus', 'sub')), may hold values from -3 to 3
- coarse_basis: float32 [2048, 8, 512], P(('clus', 'sub')), may hold values from -0.6 to 0.6
- level2_inverse: float32 [128, 128, 128], P('clus'), may hold values from -3 to 3
- level2_basis: float32 [128, 32, 128], P('clus'), may hold values from -1.5 to 1.5
- level3_inverse: float32 [4096, 4096], P('clus'), may hold values from -3 to 3
Outputs:
- preconditioned: float32 [2048, 32, 512], P(('clus', 'sub'))
All inputs are finite; a program needn't handle non-finite values.
Results may differ from a plain program's by a relative error of at most 0.00084.
Values sent between devices are 32-bit elements; how exact they have to be, the bound alone decides.
No kernel may reach another device: no remote copies, remote signals or barrier semaphores. Data moves between devices by JAX's collectives and lax.ppermute only.
A program may use at most 64 MiB of HBM per device.

v0:
```python
import jax
import jax.numpy as jnp
from jax import lax
from jax.sharding import Mesh, PartitionSpec as P

IFW = 128
SPREAD = ("x", "z", "core", "sub")


def from_behind_2(array, axis, by, only=None):
    count = lax.axis_size(axis)
    pairs = [(i, i + by) for i in range(count) if 0 <= i + by < count and (only is None or only(i))]
    return lax.ppermute(array, axis, pairs)


def couple(values_in):
    lower_rim = values_in[:, :, :IFW]
    upper_rim = values_in[:, :, values_in.shape[2] - IFW :]
    from_before = from_behind_2(upper_rim[-1:], SPREAD, 1)
    from_behind = from_behind_2(lower_rim[:1], SPREAD, -1)
    return add_rims(values_in, from_before, from_behind)


def add_rims(values_in, from_before, from_behind):
    lower_rim = values_in[:, :, :IFW]
    upper_rim = values_in[:, :, values_in.shape[2] - IFW :]
    prev_rims = jnp.concatenate([from_before, upper_rim[:-1]], 0)
    next_rims = jnp.concatenate([lower_rim[1:], from_behind], 0)
    coupled = values_in.at[:, :, :IFW].add(0.5 * prev_rims)
    return coupled.at[:, :, values_in.shape[2] - IFW :].add(0.5 * next_rims)


def rim_update(local_rim, basis_rim, coefficients):
    high = lax.Precision.HIGHEST
    return local_rim + jnp.einsum("snk,snr->srk", basis_rim, coefficients[None], precision=high)


def shards(residual_in, local_inverse, coarse_basis, level2_inverse, level2_basis, level3_inverse):
    high = lax.Precision.HIGHEST
    sub = lax.axis_size("sub")
    position = lax.axis_index("sub")
    nloc = residual_in.shape[2]
    nc = coarse_basis.shape[1]
    rhs = couple(residual_in)
    rhs_low = rhs.astype(jnp.bfloat16)
    local = jnp.einsum("srk,sjk->srj", rhs_low, local_inverse, preferred_element_type=jnp.float32)
    coarse = jnp.einsum("snk,srk->snr", coarse_basis, rhs, precision=high)
    nrhs = local.shape[1]
    first_local = local[0, :, :IFW]
    last_local = local[-1, :, nloc - IFW :]
    first_basis = coarse_basis[0, :, :IFW]
    last_basis = coarse_basis[-1, :, nloc - IFW :]
    sizes = [coarse.size, nrhs * IFW, nrhs * IFW, nc * IFW, nc * IFW]
    starts = [sum(sizes[:i]) for i in range(len(sizes) + 1)]
    packed = jnp.concatenate(
        [
            coarse.reshape(-1),
            first_local.reshape(-1),
            last_local.reshape(-1),
            first_basis.reshape(-1),
            last_basis.reshape(-1),
        ],
        0,
    )
    gathered = lax.all_gather(packed, "sub", axis=0, tiled=False)
    groups = gathered[:, : starts[1]].reshape(-1, nrhs)
    level2 = jnp.dot(level2_inverse[0], groups, precision=high)
    level3_in = jnp.dot(level2_basis[0], groups, precision=high)
    is_last = position == sub - 1
    last_fold = jnp.dot(level2_basis[0][:, -nc:].T, level3_inverse, precision=high)
    first_fold = jnp.dot(level2_basis[0][:, :nc].T, level3_inverse, precision=high)
    to_last = jnp.concatenate(
        [
            last_local.reshape(-1),
            last_basis.reshape(-1),
            last_fold.reshape(-1),
            level2[-nc:].reshape(-1),
        ],
        0,
    )
    to_first = jnp.concatenate(
        [
            first_local.reshape(-1),
            first_basis.reshape(-1),
            first_fold.reshape(-1),
            level2[:nc].reshape(-1),
        ],
        0,
    )
    outgoing = jnp.where(is_last, to_last, to_first)
    count = lax.axis_size(SPREAD)
    pairs = [(i, i + 1) for i in range(sub - 1, count - 1, sub)] + [
        (i + 1, i) for i in range(sub - 1, count - 1, sub)
    ]
    incoming = lax.ppermute(outgoing, SPREAD, pairs)
    gathered_in = level3_in
    for axis in ("core", "z", "x"):
        gathered_in = lax.all_gather(gathered_in, axis, axis=0, tiled=True)
    level3 = jnp.dot(level3_inverse, gathered_in, precision=high)
    corrected = level2 + jnp.dot(level2_basis[0].T, level3, precision=high)
    own_count = coarse.shape[0] * coarse.shape[1]
    own_rows = lax.dynamic_slice_in_dim(corrected, position * own_count, own_count, 0)
    per_sub = own_rows.reshape(coarse.shape[0], coarse.shape[1], -1)
    update = local + jnp.einsum("snk,snr->srk", coarse_basis, per_sub, precision=high)
    cut = [nrhs * IFW, nc * IFW, nc * level3_inverse.shape[1], nc * nrhs]
    at = [sum(cut[:i]) for i in range(len(cut) + 1)]
    cross_local = incoming[at[0] : at[1]].reshape(1, nrhs, IFW)
    cross_basis = incoming[at[1] : at[2]].reshape(1, nc, IFW)
    cross_fold = incoming[at[2] : at[3]].reshape(nc, -1)
    cross_rows = incoming[at[3] : at[4]].reshape(nc, nrhs)
    cross_coef = cross_rows + jnp.dot(cross_fold, gathered_in, precision=high)
    cross_rim = rim_update(cross_local, cross_basis, cross_coef)
    prev_device = lax.dynamic_index_in_dim(
        gathered, jnp.maximum(position - 1, 0), 0, keepdims=False
    )
    next_device = lax.dynamic_index_in_dim(
        gathered, jnp.minimum(position + 1, sub - 1), 0, keepdims=False
    )
    prev_rows = lax.dynamic_slice_in_dim(corrected, position * own_count - nc, nc, 0)
    next_rows = lax.dynamic_slice_in_dim(corrected, (position + 1) * own_count, nc, 0)
    inner_before = rim_update(
        prev_device[starts[2] : starts[3]].reshape(1, nrhs, IFW),
        prev_device[starts[4] : starts[5]].reshape(1, nc, IFW),
        prev_rows,
    )
    inner_behind = rim_update(
        next_device[starts[1] : starts[2]].reshape(1, nrhs, IFW),
        next_device[starts[3] : starts[4]].reshape(1, nc, IFW),
        next_rows,
    )
    from_before = jnp.where(position > 0, inner_before, cross_rim)
    from_behind = jnp.where(is_last, cross_rim, inner_behind)
    return add_rims(update, from_before, from_behind)


def solution(mesh):
    clus, sub = (mesh.shape["clus"], mesh.shape["sub"])
    x_size = 4
    z_size = clus // (2 * x_size)
    split = Mesh(mesh.devices.reshape(x_size, z_size, 2, sub), SPREAD)
    clus_axes = ("x", "z", "core")
    in_specs = (
        P(SPREAD, None, None),
        P(SPREAD, None, None),
        P(SPREAD, None, None),
        P(clus_axes, None, None),
        P(clus_axes, None, None),
        P(clus_axes, None),
    )
    out_specs = P(SPREAD, None, None)
    return jax.shard_map(
        shards, mesh=split, in_specs=in_specs, out_specs=out_specs, check_vma=False
    )
```

profile of v0, /device:TPU:2, one launch (start us, length us, event | category | flops | bytes accessed | tf_op | source)
XLA Modules:
  0.0 99.6 jit_solution(17266841809985329876)
XLA Ops:
  0.0 1.1 %copy.28 = f32[4,32,512]{2,1,0:T(8,128)S(1)} copy(f32[4,32,512]{2,1,0:T(8,128)} %param.14) | data formatting | bytes 524288
  1.1 13.3 %collective-permute-start.1 = (f32[1,32,128]{2,1,0:T(8,128)S(1)}, f32[1,32,128]{2,1,0:T(8,128)S(1)}, u32[]{:S(2)}, u32[]{:S(2)}) collective-permute-start(f32[1,32,128]{2,1,0:T(8,128)S(1)} %get-tuple-element.59), channel_id=1, source_target_pairs={{1,0},{2,1},{3,2},{4,3},{5,4},{6,5},{7,6},{8,7},{9,8},{10,9},{11,1... | collective-permute-start | bytes 49160 | tf_op jit(solution)/shard_map/ppermute | solution.py:13
  14.4 1.9 %collective-permute-start = (f32[1,32,128]{2,1,0:T(8,128)S(1)}, f32[1,32,128]{2,1,0:T(8,128)S(1)}, u32[]{:S(2)}, u32[]{:S(2)}) collective-permute-start(f32[1,32,128]{2,1,0:T(8,128)S(1)} %get-tuple-element.60), channel_id=1, source_target_pairs={{0,1},{1,2},{2,3},{3,4},{4,5},{5,6},{6,7},{7,8},{8,9},{9,10},{10,1... | collective-permute-start | bytes 49160 | tf_op jit(solution)/shard_map/ppermute | solution.py:13
  16.3 1.3 %slice_bitcast_fusion.6 = (f32[1024]{0:T(1024)}, f32[1024]{0:T(1024)}) fusion(f32[4,8,512]{2,1,0:T(8,128)} %param.16), kind=kLoop, calls=%fused_computation.44 | loop fusion | bytes 16384 | tf_op jit(solution)/shard_map/reshape;squeeze | solution.py:60
  17.6 1.4 %convolution_bitcast_fusion = f32[1,32,8,128]{3,2,1,0:T(8,128)S(1)} fusion(f32[32,4096]{1,0:T(8,128)} %param.19, f32[32,128]{1,0:T(8,128)} %bitcast.82), kind=kOutput, calls=%fused_computation.1 | convolution fusion | flops 12582912 | bytes 671744 | tf_op jit(solution)/shard_map/dot_general | solution.py:71
  19.1 1.5 %convolution_bitcast_fusion.1 = f32[1,32,8,128]{3,2,1,0:T(8,128)S(1)} fusion(f32[32,4096]{1,0:T(8,128)} %param.19, f32[32,128]{1,0:T(8,128)} %bitcast.83), kind=kOutput, calls=%fused_computation.2 | convolution fusion | flops 12582912 | bytes 671744 | tf_op jit(solution)/shard_map/dot_general | solution.py:70
  20.7 3.0 %collective-permute-done = f32[1,32,128]{2,1,0:T(8,128)S(1)} collective-permute-done((f32[1,32,128]{2,1,0:T(8,128)S(1)}, f32[1,32,128]{2,1,0:T(8,128)S(1)}, u32[]{:S(2)}, u32[]{:S(2)}) %collective-permute-start) | collective-permute-done | bytes 16416 | tf_op jit(solution)/shard_map/ppermute | solution.py:13
  23.7 0.3 convolution_bitcast_fusion.5
  24.1 0.7 fusion.5
  24.9 12.2 %all-gather = f32[45056]{0:T(1024)S(1)} all-gather(f32[11264]{0:T(1024)S(1)} %constant_dynamic-update-slice_fusion.1), channel_id=2, replica_groups=mesh['x'=4,'z'=16,'core'=2,'sub'=4] {'sub'}, dimensions={0}, use_global_device_ids=true | all-gather | bytes 225280 | tf_op jit(solution)/shard_map/all_gather | solution.py:65
  37.2 0.7 reshape.223
  37.9 0.7 slice.239
  38.7 0.2 convolution_bitcast_fusion.3
  39.0 1.1 %convolution_bitcast_fusion.4 = f32[128,32]{0,1:T(8,128)S(1)} fusion(f32[128,32]{1,0:T(8,128)S(1)} %reshape.211, f32[1,128,128]{2,1,0:T(8,128)} %param.17), kind=kOutput, calls=%fused_computation.12 | convolution fusion | flops 6291456 | bytes 98304 | tf_op jit(solution)/shard_map/dot_general | solution.py:67
  40.2 1.8 %all_gather.17 = f32[64,32]{1,0:T(8,128)S(1)} all-gather(f32[32,32]{1,0:T(8,128)S(1)} %copy.11), channel_id=1, replica_groups=mesh['x'=4,'z'=16,'core'=2,'sub'=4] {'core'}, dimensions={0}, use_global_device_ids=true | all-gather | bytes 12288 | tf_op jit(solution)/shard_map/all_gather | solution.py:98
  42.4 1.4 %maximum_select_fusion = f32[38144]{0:T(1024)} fusion(f32[256]{0:T(256)S(1)} %reshape.216, f32[32768]{0:T(1024)S(1)} %bitcast.81, f32[1024]{0:T(1024)} %get-tuple-element.66, f32[4096]{0:T(1024)S(1)} %get-tuple-element.56, f32[256]{0:T(256)S(1)} %reshape.218, f32[32768]{0:T(1024)S(1)} %bitcast.80, f32[1024]{0:T(1024)} %get-tuple-element.65, ...), kind=kLoop, calls=%fused_computation.14 | loop fusion | flops 267008 | bytes 457729 | tf_op jit(solution)/shard_map/jit(_where)/select_n | solution.py:90
  43.8 2.3 %collective-permute-start.2 = (f32[38144]{0:T(1024)}, f32[38144]{0:T(1024)}, u32[]{:S(2)}, u32[]{:S(2)}) collective-permute-start(f32[38144]{0:T(1024)} %maximum_select_fusion), channel_id=1, source_target_pairs={{3,4},{7,8},{11,12},{15,16},{19,20},{23,24},{27,28},{31,32},{35,36... | collective-permute-start | bytes 457736 | tf_op jit(solution)/shard_map/ppermute | solution.py:95
  46.1 28.7 %all-gather.1 = f32[16,64,32]{1,2,0:T(8,128)S(1)} all-gather(f32[1,64,32]{1,2,0:T(8,128)S(1)} %copy.12), channel_id=1, replica_groups=mesh['x'=4,'z'=16,'core'=2,'sub'=4] {'z'}, dimensions={0}, use_global_device_ids=true | all-gather | bytes 139264 | tf_op jit(solution)/shard_map/all_gather | solution.py:98
  74.8 0.2 copy.13
  75.1 13.1 %all_gather.19 = f32[4096,32]{0,1:T(8,128)S(1)} all-gather(f32[1024,32]{0,1:T(8,128)S(1)} %reshape.225), channel_id=1, replica_groups=mesh['x'=4,'z'=16,'core'=2,'sub'=4] {'x'}, dimensions={0}, use_global_device_ids=true | all-gather | bytes 655360 | tf_op jit(solution)/shard_map/all_gather | solution.py:98
  88.3 0.5 fusion.31
  88.8 0.9 fusion.4
  89.8 1.3 %convolution_add_fusion = f32[4,32,512]{2,1,0:T(8,128)S(1)} fusion(f32[4,32,512]{2,1,0:T(8,128)S(1)} %fusion.5, f32[4,8,512]{2,1,0:T(8,128)} %param.16, f32[32,32]{1,0:T(8,128)S(1)} %copy.14), kind=kOutput, calls=%fused_computation | convolution fusion | flops 6356992 | bytes 593920 | tf_op jit(solution)/shard_map/snk,snr->srk/dot_general | solution.py:104
  91.1 1.0 %fusion.29 = (f32[1,4096]{1,0:T(1,128)S(1)}, f32[1,4096]{1,0:T(1,128)S(1)}) fusion(f32[4,11264]{1,0:T(4,128)} %reshape.223, s32[]{:T(128)S(6)} %select_n.50, s32[]{:T(128)S(6)} %add.88, s32[]{:T(128)S(6)} %max.3, s32[]{:T(128)S(6)} %add.86), kind=kLoop, calls=%fused_computation.58 | loop fusion | bytes 65552 | tf_op jit(solution)/shard_map/slice | solution.py:127
  92.1 0.8 fusion.28
  93.0 0.7 slice.246
  93.7 0.9 slice.247
  94.7 0.5 fusion.32
  95.2 0.9 fusion.19
  96.1 0.9 fusion.3
  97.1 1.0 fusion.1
  98.1 1.5 %fusion.7 = f32[4,32,512]{2,1,0:T(8,128)} fusion(f32[4,32,512]{2,1,0:T(8,128)} %copy-done.2, f32[1,32,128]{2,1,0:T(8,128)S(1)} %fusion.1, f32[3,32,128]{2,1,0:T(8,128)S(1)} %get-tuple-element.53), kind=kLoop, calls=%fused_computation.18 | loop fusion | flops 49152 | bytes 196608 | tf_op jit(solution)/shard_map/scatter-add | solution.py:30
  (40 shorter events, 1.3 us)
Async XLA Ops:
  0.0 24.1 %copy-start = (bf16[4,512,512]{2,1,0:T(8,128)(2,1)S(1)}, bf16[4,512,512]{2,1,0:T(8,128)(2,1)}, u32[]{:S(2)}) copy-start(bf16[4,512,512]{2,1,0:T(8,128)(2,1)} %param.15) | copy-start | bytes 6291460
  0.0 23.7 %copy-start.3 = (f32[4,8,512]{2,1,0:T(8,128)S(1)}, f32[4,8,512]{2,1,0:T(8,128)}, u32[]{:S(2)}) copy-start(f32[4,8,512]{2,1,0:T(8,128)} %param.16) | copy-start | bytes 196612
  1.1 22.6 %collective-permute-start.1 = (f32[1,32,128]{2,1,0:T(8,128)S(1)}, f32[1,32,128]{2,1,0:T(8,128)S(1)}, u32[]{:S(2)}, u32[]{:S(2)}) collective-permute-start(f32[1,32,128]{2,1,0:T(8,128)S(1)} %get-tuple-element.59), channel_id=1, source_target_pairs={{1,0},{2,1},{3,2},{4,3},{5,4},{6,5},{7,6},{8,7},{9,8},{10,9},{11,1... | collective-permute-start | bytes 49160 | tf_op jit(solution)/shard_map/ppermute | solution.py:13
  14.4 9.3 %collective-permute-start = (f32[1,32,128]{2,1,0:T(8,128)S(1)}, f32[1,32,128]{2,1,0:T(8,128)S(1)}, u32[]{:S(2)}, u32[]{:S(2)}) collective-permute-start(f32[1,32,128]{2,1,0:T(8,128)S(1)} %get-tuple-element.60), channel_id=1, source_target_pairs={{0,1},{1,2},{2,3},{3,4},{4,5},{5,6},{6,7},{7,8},{8,9},{9,10},{10,1... | collective-permute-start | bytes 49160 | tf_op jit(solution)/shard_map/ppermute | solution.py:13
  23.7 15.1 %copy-start.4 = (f32[1,32,128]{2,1,0:T(8,128)S(1)}, f32[1,32,128]{2,1,0:T(8,128)}, u32[]{:S(2)}) copy-start(f32[1,32,128]{2,1,0:T(8,128)} %param.18) | copy-start | bytes 49156
  24.9 63.4 %copy-start.1 = (f32[32,4096]{1,0:T(8,128)S(1)}, f32[32,4096]{1,0:T(8,128)}, u32[]{:S(2)}) copy-start(f32[32,4096]{1,0:T(8,128)} %param.19) | copy-start | bytes 1572868
  43.8 49.2 %collective-permute-start.2 = (f32[38144]{0:T(1024)}, f32[38144]{0:T(1024)}, u32[]{:S(2)}, u32[]{:S(2)}) collective-permute-start(f32[38144]{0:T(1024)} %maximum_select_fusion), channel_id=1, source_target_pairs={{3,4},{7,8},{11,12},{15,16},{19,20},{23,24},{27,28},{31,32},{35,36... | collective-permute-start | bytes 457736 | tf_op jit(solution)/shard_map/ppermute | solution.py:95
  97.1 1.0 %copy-start.2 = (f32[4,32,512]{2,1,0:T(8,128)}, f32[4,32,512]{2,1,0:T(8,128)S(1)}, u32[]{:S(2)}) copy-start(f32[4,32,512]{2,1,0:T(8,128)S(1)} %fusion.8) | copy-start | bytes 786436
where the time goes:
time: 101 us; the launch traced here: 99.6 us
  blocking collectives  55.9 us (55%)
  starting transfers between devices  17.5 us (17%)
  matrix products  11.3 us (11%)
  local copies, waits for them, and re-layouts  8.68 us (9%)
  waiting for transfers between devices  2.96 us (3%)
  other arithmetic  2.92 us (3%)
    all_gather x3, blocking collectives, shards(): gathered_in = lax.all_gather(gathered_in, axis, axis=0, tiled=True)  43.6 us
    ppermute x2, starting transfers between devices, from_behind_2(): return lax.ppermute(array, axis, pairs)  15.2 us
    all_gather x1, blocking collectives, shards(): gathered = lax.all_gather(packed, 'sub', axis=0, tiled=False)  12.2 us
    ppermute x2, waiting for transfers between devices, from_behind_2(): return lax.ppermute(array, axis, pairs)  2.96 us
    dot_general x3, matrix products, rim_update(): jnp.einsum('snk,snr->srk', basis_rim, coefficients[None], precision=high)  2.81 us
    ppermute x1, starting transfers between devices, shards(): incoming = lax.ppermute(outgoing, SPREAD, pairs)  2.34 us
  transfers between devices with their start and end apart: 3, of which 1 were waited for; matrix products, arithmetic and copies ran while one was open for 9% of the time, Pallas kernels for 0%

commit v1 on v0

--- a/solution.py
+++ b/solution.py
@@ -95,7 +95,9 @@
     incoming = lax.ppermute(outgoing, SPREAD, pairs)
     gathered_in = level3_in
     for axis in ("core", "z", "x"):
-        gathered_in = lax.all_gather(gathered_in, axis, axis=0, tiled=True)
+        gathered_in = jnp.concatenate(
+            lax.all_to_all(jnp.stack([gathered_in] * lax.axis_size(axis)), axis, 0, 0), axis=0
+        )
     level3 = jnp.dot(level3_inverse, gathered_in, precision=high)
     corrected = level2 + jnp.dot(level2_basis[0].T, level3, precision=high)
     own_count = coarse.shape[0] * coarse.shape[1]

time: 101 us -> 88.6 us (0.88)
  the two profiles are of different devices: /device:TPU:2 before, /device:TPU:32 now
where the time goes in v1:
time: 88.6 us; the launch traced here: 87.4 us
  starting transfers between devices  30.4 us (34%)
  blocking collectives  15.8 us (18%)
  local copies, waits for them, and re-layouts  14.4 us (16%)
  waiting for transfers between devices  12.8 us (14%)
  matrix products  9.82 us (11%)
  other arithmetic  3.74 us (4%)
    all_to_all x2, starting transfers between devices, shards(): lax.all_to_all(jnp.stack([gathered_in] * lax.axis_size(axis)), axis, 0, 0)  20.8 us
    all_to_all x2, waiting for transfers between devices, shards(): lax.all_to_all(jnp.stack([gathered_in] * lax.axis_size(axis)), axis, 0, 0)  12.8 us
    all_gather x1, blocking collectives, shards(): gathered = lax.all_gather(packed, 'sub', axis=0, tiled=False)  12.1 us
    ppermute x2, starting transfers between devices, from_behind_2(): return lax.ppermute(array, axis, pairs)  7.66 us
    all_to_all x1, blocking collectives, shards(): lax.all_to_all(jnp.stack([gathered_in] * lax.axis_size(axis)), axis, 0, 0)  3.71 us
    unnamed x30, local copies, waits for them, and re-layouts  3.2 us
    dot_general x3, matrix products, rim_update(): jnp.einsum('snk,snr->srk', basis_rim, coefficients[None], precision=high)  2.9 us
    ppermute x1, starting transfers between devices, shards(): incoming = lax.ppermute(outgoing, SPREAD, pairs)  1.91 us
  transfers between devices with their start and end apart: 5, of which 2 were waited for; matrix products, arithmetic and copies ran while one was open for 16% of the time, Pallas kernels for 0%

profile of v1, /device:TPU:32, one launch (start us, length us, event | category | flops | bytes accessed | tf_op | source)
XLA Modules:
  0.0 87.4 jit_solution(3638430913077354602)
XLA Ops:
  0.0 1.1 %copy.34 = f32[4,32,512]{2,1,0:T(8,128)S(1)} copy(f32[4,32,512]{2,1,0:T(8,128)} %param.14) | data formatting | bytes 524288
  1.1 3.5 %collective-permute-start = (f32[1,32,128]{2,1,0:T(8,128)S(1)}, f32[1,32,128]{2,1,0:T(8,128)S(1)}, u32[]{:S(2)}, u32[]{:S(2)}) collective-permute-start(f32[1,32,128]{2,1,0:T(8,128)S(1)} %get-tuple-element.60), channel_id=1, source_target_pairs={{0,1},{1,2},{2,3},{3,4},{4,5},{5,6},{6,7},{7,8},{8,9},{9,10},{10,1... | collective-permute-start | bytes 49160 | tf_op jit(solution)/shard_map/ppermute | solution.py:13
  4.6 4.2 %collective-permute-start.1 = (f32[1,32,128]{2,1,0:T(8,128)S(1)}, f32[1,32,128]{2,1,0:T(8,128)S(1)}, u32[]{:S(2)}, u32[]{:S(2)}) collective-permute-start(f32[1,32,128]{2,1,0:T(8,128)S(1)} %get-tuple-element.59), channel_id=1, source_target_pairs={{1,0},{2,1},{3,2},{4,3},{5,4},{6,5},{7,6},{8,7},{9,8},{10,9},{11,1... | collective-permute-start | bytes 49160 | tf_op jit(solution)/shard_map/ppermute | solution.py:13
  8.8 0.7 slice_bitcast_fusion.6
  9.5 1.5 %convolution_bitcast_fusion.1 = f32[1,32,8,128]{3,2,1,0:T(8,128)S(1)} fusion(f32[32,4096]{1,0:T(8,128)} %param.19, f32[32,128]{1,0:T(8,128)} %bitcast.97), kind=kOutput, calls=%fused_computation.2 | convolution fusion | flops 12582912 | bytes 671744 | tf_op jit(solution)/shard_map/dot_general | solution.py:70
  11.0 1.4 %convolution_bitcast_fusion = f32[1,32,8,128]{3,2,1,0:T(8,128)S(1)} fusion(f32[32,4096]{1,0:T(8,128)} %param.19, f32[32,128]{1,0:T(8,128)} %bitcast.98), kind=kOutput, calls=%fused_computation.1 | convolution fusion | flops 12582912 | bytes 671744 | tf_op jit(solution)/shard_map/dot_general | solution.py:71
  13.0 0.7 fusion.5
  13.9 12.1 %all-gather = f32[45056]{0:T(1024)S(1)} all-gather(f32[11264]{0:T(1024)S(1)} %constant_dynamic-update-slice_fusion.1), channel_id=2, replica_groups=mesh['x'=4,'z'=16,'core'=2,'sub'=4] {'sub'}, dimensions={0}, use_global_device_ids=true | all-gather | bytes 225280 | tf_op jit(solution)/shard_map/all_gather | solution.py:65
  26.8 3.7 %all_to_all.15 = f32[2,1,1024]{2,1,0:T(1,128)S(1)} all-to-all(f32[2,1,1024]{2,1,0:T(1,128)S(1)} %reshape.232), channel_id=1, replica_groups=mesh['x'=4,'z'=16,'core'=2,'sub'=4] {'core'}, dimensions={0} | all-to-all | bytes 16384 | tf_op jit(solution)/shard_map/all_to_all | solution.py:99
  31.0 0.6 reduce.8
  31.9 0.9 reshape.234
  32.7 16.5 %all-to-all-start.1 = ((f32[16,1,2048]{2,1,0:T(1,128)}), f32[16,1,2048]{2,1,0:T(1,128)S(1)}, u32[]{:S(2)}, u32[]{:S(2)}) async-start(f32[16,1,2048]{2,1,0:T(1,128)} %reshape.234), calls=%async_computation.1 | async-start | bytes 262144 | tf_op jit(solution)/shard_map/all_to_all | solution.py:99
  49.6 0.7 maximum_select_fusion
  50.3 1.9 %collective-permute-start.2 = (f32[38144]{0:T(1024)}, f32[38144]{0:T(1024)}, u32[]{:S(2)}, u32[]{:S(2)}) collective-permute-start(f32[38144]{0:T(1024)} %maximum_select_fusion), channel_id=1, source_target_pairs={{3,4},{7,8},{11,12},{15,16},{19,20},{23,24},{27,28},{31,32},{35,36... | collective-permute-start | bytes 457736 | tf_op jit(solution)/shard_map/ppermute | solution.py:95
  52.2 10.9 %all-to-all-done.1 = f32[16,1,2048]{2,1,0:T(1,128)S(1)} async-done(((f32[16,1,2048]{2,1,0:T(1,128)}), f32[16,1,2048]{2,1,0:T(1,128)S(1)}, u32[]{:S(2)}, u32[]{:S(2)}) %all-to-all-start.1) | async-done | bytes 131104 | tf_op jit(solution)/shard_map/all_to_all | solution.py:99
  63.1 0.9 %reduce.9 = f32[16,2048]{1,0:T(8,128)S(1)} reduce(f32[16,1,2048]{2,1,0:T(1,128)S(1)} %all-to-all-done.1, f32[]{:T(128)} %broadcast.72), dimensions={1}, to_apply=%all_to_all.10.reduce_sub_computation | reduce | bytes 262148 | tf_op jit(solution)/shard_map/all_to_all | solution.py:99
  64.4 0.9 stack.16
  65.3 4.3 %all-to-all-start.2 = ((f32[4,1024,32]{1,2,0:T(8,128)}), f32[4,1024,32]{1,2,0:T(8,128)S(1)}, u32[]{:S(2)}, u32[]{:S(2)}) async-start(f32[4,1024,32]{1,2,0:T(8,128)} %stack.16), calls=%async_computation.2 | async-start | bytes 1048576 | tf_op jit(solution)/shard_map/all_to_all | solution.py:99
  69.6 1.6 %fusion.29 = (f32[1,4096]{1,0:T(1,128)}, f32[1,4096]{1,0:T(1,128)}) fusion(f32[4,11264]{1,0:T(4,128)} %copy-done.5, s32[]{:T(128)S(6)} %select_n.50, s32[]{:T(128)S(6)} %add.88, s32[]{:T(128)S(6)} %max.3, s32[]{:T(128)S(6)} %add.86), kind=kLoop, calls=%fused_computation.59 | loop fusion | bytes 65552 | tf_op jit(solution)/shard_map/slice | solution.py:129
  71.2 1.4 %fusion.28 = (f32[1,1024]{1,0:T(1,128)}, f32[1,1024]{1,0:T(1,128)}) fusion(f32[4,11264]{1,0:T(4,128)} %copy-done.5, s32[]{:T(128)S(6)} %select_n.50, s32[]{:T(128)S(6)} %add.89, s32[]{:T(128)S(6)} %max.3, s32[]{:T(128)S(6)} %add.87), kind=kLoop, calls=%fused_computation.58 | loop fusion | bytes 16400 | tf_op jit(solution)/shard_map/slice | solution.py:130
  72.6 0.7 slice.246
  73.3 0.7 reshape.227
  74.0 1.6 %slice.247 = f32[32768]{0:T(1024)} slice(f32[38144]{0:T(1024)} %collective-permute-done.2), slice={[5120:37888]} | slice | bytes 262144 | tf_op jit(solution)/shard_map/slice | solution.py:111
  75.5 0.9 %reshape.228 = f32[8,4096]{1,0:T(8,128)S(1)} reshape(f32[32768]{0:T(1024)} %slice.247) | data formatting | bytes 262144 | tf_op jit(solution)/shard_map/reshape | solution.py:111
  76.5 1.9 %all-to-all-done.2 = f32[4,1024,32]{1,2,0:T(8,128)S(1)} async-done(((f32[4,1024,32]{1,2,0:T(8,128)}), f32[4,1024,32]{1,2,0:T(8,128)S(1)}, u32[]{:S(2)}, u32[]{:S(2)}) %all-to-all-start.2) | async-done | bytes 524320 | tf_op jit(solution)/shard_map/all_to_all | solution.py:99
  78.4 0.8 copy-done.2
  79.2 1.1 %copy.22 = f32[4,4,8,1024]{3,2,0,1:T(8,128)S(1)} copy(f32[4,4,8,1024]{3,2,1,0:T(8,128)} %bitcast.93) | data formatting | bytes 1048576 | tf_op jit(solution)/shard_map/reshape | solution.py:98
  81.2 1.3 %convolution_add_fusion = f32[4,32,512]{2,1,0:T(8,128)S(1)} fusion(f32[4,32,512]{2,1,0:T(8,128)S(1)} %fusion.5, f32[4,8,512]{2,1,0:T(8,128)} %param.16, f32[32,32]{1,0:T(8,128)S(1)} %copy.19), kind=kOutput, calls=%fused_computation | convolution fusion | flops 6356992 | bytes 593920 | tf_op jit(solution)/shard_map/snk,snr->srk/dot_general | solution.py:106
  83.0 0.9 %fusion.19 = f32[32,128]{1,0:T(8,128)S(1)} fusion(f32[38144]{0:T(1024)} %collective-permute-done.2, f32[8,32]{1,0:T(8,128)} %reshape.227, f32[8,32]{1,0:T(8,128)S(1)} %fusion.33), kind=kOutput, calls=%fused_computation.41 | convolution fusion | flops 393472 | bytes 25600 | tf_op jit(solution)/shard_map/snk,snr->srk/dot_general | solution.py:35
  83.9 1.0 %fusion.3 = f32[1,32,128]{2,1,0:T(8,128)S(1)} fusion(f32[32,128]{1,0:T(8,128)} %bitcast.101, f32[8,128]{1,0:T(8,128)} %bitcast.103, f32[128,32]{0,1:T(8,128)S(1)} %fusion.4, s32[]{:T(128)S(6)} %select_n.44, pred[]{:T(512)S(6)} %gt.3, f32[32,128]{1,0:T(8,128)S(1)} %fusion.19, f32[38144]{0:T(1024)} %collective-permute-done.2), kind=kOutput, calls=%fused_computation.8 | convolution fusion | flops 405504 | bytes 86021 | tf_op jit(solution)/shard_map/snk,snr->srk/dot_general | solution.py:35
  84.9 1.0 %fusion.1 = f32[1,32,128]{2,1,0:T(8,128)S(1)} fusion(f32[32,128]{1,0:T(8,128)} %bitcast.100, f32[8,128]{1,0:T(8,128)} %bitcast.102, f32[128,32]{0,1:T(8,128)S(1)} %fusion.4, s32[]{:T(128)S(6)} %select_n.51, pred[]{:T(512)S(6)} %eq.3, f32[32,128]{1,0:T(8,128)S(1)} %fusion.19, f32[38144]{0:T(1024)} %collective-permute-done.2), kind=kOutput, calls=%fused_computation.5 | convolution fusion | flops 405504 | bytes 86021 | tf_op jit(solution)/shard_map/snk,snr->srk/dot_general | solution.py:35
  86.0 1.5 %fusion.7 = f32[4,32,512]{2,1,0:T(8,128)} fusion(f32[4,32,512]{2,1,0:T(8,128)} %copy-done.3, f32[1,32,128]{2,1,0:T(8,128)S(1)} %fusion.1, f32[3,32,128]{2,1,0:T(8,128)S(1)} %get-tuple-element.53), kind=kLoop, calls=%fused_computation.18 | loop fusion | flops 49152 | bytes 196608 | tf_op jit(solution)/shard_map/scatter-add | solution.py:30
  (61 shorter events, 4.2 us)
Async XLA Ops:
  0.0 13.0 %copy-start = (bf16[4,512,512]{2,1,0:T(8,128)(2,1)S(1)}, bf16[4,512,512]{2,1,0:T(8,128)(2,1)}, u32[]{:S(2)}) copy-start(bf16[4,512,512]{2,1,0:T(8,128)(2,1)} %param.15) | copy-start | bytes 6291460
  0.0 12.7 %copy-start.4 = (f32[4,8,512]{2,1,0:T(8,128)S(1)}, f32[4,8,512]{2,1,0:T(8,128)}, u32[]{:S(2)}) copy-start(f32[4,8,512]{2,1,0:T(8,128)} %param.16) | copy-start | bytes 196612
  1.1 11.5 %collective-permute-start = (f32[1,32,128]{2,1,0:T(8,128)S(1)}, f32[1,32,128]{2,1,0:T(8,128)S(1)}, u32[]{:S(2)}, u32[]{:S(2)}) collective-permute-start(f32[1,32,128]{2,1,0:T(8,128)S(1)} %get-tuple-element.60), channel_id=1, source_target_pairs={{0,1},{1,2},{2,3},{3,4},{4,5},{5,6},{6,7},{7,8},{8,9},{9,10},{10,1... | collective-permute-start | bytes 49160 | tf_op jit(solution)/shard_map/ppermute | solution.py:13
  4.6 8.1 %collective-permute-start.1 = (f32[1,32,128]{2,1,0:T(8,128)S(1)}, f32[1,32,128]{2,1,0:T(8,128)S(1)}, u32[]{:S(2)}, u32[]{:S(2)}) collective-permute-start(f32[1,32,128]{2,1,0:T(8,128)S(1)} %get-tuple-element.59), channel_id=1, source_target_pairs={{1,0},{2,1},{3,2},{4,3},{5,4},{6,5},{7,6},{8,7},{9,8},{10,9},{11,1... | collective-permute-start | bytes 49160 | tf_op jit(solution)/shard_map/ppermute | solution.py:13
  12.6 13.6 %copy-start.6 = (f32[1,32,128]{2,1,0:T(8,128)S(1)}, f32[1,32,128]{2,1,0:T(8,128)}, u32[]{:S(2)}) copy-start(f32[1,32,128]{2,1,0:T(8,128)} %param.18) | copy-start | bytes 49156
  12.6 13.8 %copy-start.8 = (f32[1,128,128]{2,1,0:T(8,128)S(1)}, f32[1,128,128]{2,1,0:T(8,128)}, u32[]{:S(2)}) copy-start(f32[1,128,128]{2,1,0:T(8,128)} %param.17) | copy-start | bytes 196612
  26.1 5.7 %copy-start.5 = (f32[4,11264]{1,0:T(4,128)}, f32[4,11264]{1,0:T(4,128)S(1)}, u32[]{:S(2)}) copy-start(f32[4,11264]{1,0:T(4,128)S(1)} %reshape.231) | copy-start | bytes 540676
  32.7 30.4 %all-to-all-start.1 = ((f32[16,1,2048]{2,1,0:T(1,128)}), f32[16,1,2048]{2,1,0:T(1,128)S(1)}, u32[]{:S(2)}, u32[]{:S(2)}) async-start(f32[16,1,2048]{2,1,0:T(1,128)} %reshape.234), calls=%async_computation.1 | async-start | bytes 262144 | tf_op jit(solution)/shard_map/all_to_all | solution.py:99
  50.3 22.3 %collective-permute-start.2 = (f32[38144]{0:T(1024)}, f32[38144]{0:T(1024)}, u32[]{:S(2)}, u32[]{:S(2)}) collective-permute-start(f32[38144]{0:T(1024)} %maximum_select_fusion), channel_id=1, source_target_pairs={{3,4},{7,8},{11,12},{15,16},{19,20},{23,24},{27,28},{31,32},{35,36... | collective-permute-start | bytes 457736 | tf_op jit(solution)/shard_map/ppermute | solution.py:95
  64.1 16.2 %copy-start.1 = (f32[32,4096]{1,0:T(8,128)S(1)}, f32[32,4096]{1,0:T(8,128)}, u32[]{:S(2)}) copy-start(f32[32,4096]{1,0:T(8,128)} %param.19) | copy-start | bytes 1572868
  65.3 13.1 %all-to-all-start.2 = ((f32[4,1024,32]{1,2,0:T(8,128)}), f32[4,1024,32]{1,2,0:T(8,128)S(1)}, u32[]{:S(2)}, u32[]{:S(2)}) async-start(f32[4,1024,32]{1,2,0:T(8,128)} %stack.16), calls=%async_computation.2 | async-start | bytes 1048576 | tf_op jit(solution)/shard_map/all_to_all | solution.py:99
  78.4 0.8 copy-start.2
  79.2 1.7 %copy-start.7 = (f32[1,32,128]{2,1,0:T(8,128)S(1)}, f32[1,32,128]{2,1,0:T(8,128)}, u32[]{:S(2)}) copy-start(f32[1,32,128]{2,1,0:T(8,128)} %param.18) | copy-start | bytes 49156
  84.9 1.1 %copy-start.3 = (f32[4,32,512]{2,1,0:T(8,128)}, f32[4,32,512]{2,1,0:T(8,128)S(1)}, u32[]{:S(2)}) copy-start(f32[4,32,512]{2,1,0:T(8,128)S(1)} %fusion.8) | copy-start | bytes 786436
